TPU v7x, 256 devices: a whole 4x4x8 slice. The times are simulated.
256 devices in a mesh: section: 2 (over core), patch: 4 (over y), req: 32 (over z, x).
Axes of the slice: x: 4, y: 4, z: 8, core: 2. Of those that a mesh axis runs over, the one named last changes fastest.
Arguments:
- hidden: bfloat16 [64, 1024, 1536], P('req', 'patch'), may hold values from -6 to 6
- w_qkv: bfloat16 [2, 1536, 2304], P('section', ('patch', 'req')), may hold values from -0.15625 to 0.15625
- w_out: bfloat16 [2, 768, 1536], P('section', ('patch', 'req')), may hold values from -0.21875 to 0.21875
- modulation: float32 [2, 64, 3, 1536], P('section', 'req'), may hold values from -3 to 3
- text_kv: bfloat16 [2, 64, 160, 1536], P('section', 'req'), may hold values from -1000 to 1000
- text_lengths: int32 [64], P('req'), may hold values from 77 to 154, as said below
- stale_kv: bfloat16 [2, 64, 1024, 1536], P('section', 'req', 'patch'), may hold values from -48 to 48
- held_hidden: bfloat16 [2, 64, 96, 1536], P('section', 'req', 'patch'), may hold values from -6 to 6
- recompute_rows: int32 [2, 64, 96], P('section', 'req', 'patch'), may hold values from 0 to 255, as said below
- coefficients: float32 [64, 2], P('req'), may hold values from 0.5 to 1.5
Outputs:
- latents: float32 [64, 1024, 1536], P('req', 'patch', 'section')
- cache: bfloat16 [2, 64, 1024, 1536], P('section', 'req', 'patch')
Inputs may be any that keep to these rules, and one draw needn't show every extreme that they name: `text_lengths`: some request has exactly 154 text tokens and some exactly 77. `recompute_rows`: the row numbers listed for one layer, request and patch are distinct.
All inputs are finite; a program needn't handle non-finite values.
Results may differ from a plain program's by a relative error of at most 0.025.
Values may be sent and summed in bfloat16 or wider, within the bound.
No kernel may reach another device: no remote copies, remote signals or barrier semaphores. Data moves between devices by JAX's collectives and lax.ppermute only.
A program may use at most 128 MiB of HBM per device.

v0:
```python
import jax
import jax.numpy as jnp
from jax import lax
from jax.sharding import PartitionSpec as P

HEADS = 12
norm_eps = 1e-06
score_scale = 0.125


def shifted(block, axis, distance):
    devices = range(lax.axis_size(axis))
    route = [(i - distance, i) for i in devices if i - distance in devices]
    return lax.ppermute(block, axis, route)


def modulate(row_block, shift_row, scale_row):
    values = row_block.astype(jnp.float32)
    centre = values - jnp.mean(values, axis=-1, keepdims=True)
    spread = jnp.mean(centre * centre, axis=-1, keepdims=True)
    return (centre * lax.rsqrt(spread + norm_eps) * (1.0 + scale_row) + shift_row).astype(
        jnp.bfloat16
    )


def attend(queries, key_rows, value_rows, usable):
    row_count = queries.shape[0]
    feature_count = queries.shape[1]
    query_heads = queries.reshape(row_count, HEADS, feature_count // HEADS)
    key_heads = key_rows.reshape(key_rows.shape[0], HEADS, feature_count // HEADS)
    value_heads = value_rows.reshape(value_rows.shape[0], HEADS, feature_count // HEADS)
    scores = (
        jnp.einsum("qhd,khd->hqk", query_heads, key_heads, preferred_element_type=jnp.float32)
        * score_scale
    )
    scores = jnp.where(usable[None, None, :], scores, -1e30)
    row_max = jnp.max(scores, axis=-1, keepdims=True)
    exp_scores = jnp.exp(scores - row_max)
    soft_weights = (exp_scores / jnp.sum(exp_scores, axis=-1, keepdims=True)).astype(jnp.bfloat16)
    attended = jnp.einsum(
        "hqk,khd->qhd", soft_weights, value_heads, preferred_element_type=jnp.float32
    )
    return attended.reshape(row_count, feature_count).astype(jnp.bfloat16)


def body(
    hidden,
    w_qkv,
    w_out,
    modulation,
    text_kv,
    text_lengths,
    stale_kv,
    held_hidden,
    recompute_rows,
    coefficients,
):
    full_qkv, full_out = (
        lax.all_gather(w_qkv[0], ("patch", "req"), axis=0, tiled=True),
        lax.all_gather(w_out[0], ("patch", "req"), axis=0, tiled=True),
    )
    section_index = lax.axis_index("section")
    patch_index = lax.axis_index("patch")
    request_count = hidden.shape[0]
    patch_rows = hidden.shape[1]
    model_width = hidden.shape[2]
    head_width = full_out.shape[0]
    text_slots = text_kv.shape[2]

    def process(layer_input, slot_index):
        mod_rows = lax.dynamic_index_in_dim(modulation[0], slot_index, 0, keepdims=False)
        text_rows = lax.dynamic_index_in_dim(text_kv[0], slot_index, 0, keepdims=False)
        text_count = lax.dynamic_index_in_dim(text_lengths, slot_index, 0, keepdims=False)
        stale_block = lax.dynamic_index_in_dim(stale_kv[0], slot_index, 0, keepdims=False)
        held_rows = lax.dynamic_index_in_dim(held_hidden[0], slot_index, 0, keepdims=False)
        redo_index = lax.dynamic_index_in_dim(recompute_rows[0], slot_index, 0, keepdims=False)
        held_norm = modulate(held_rows, mod_rows[0], mod_rows[1])
        redone = jnp.dot(
            held_norm, full_qkv[:, head_width:], preferred_element_type=jnp.float32
        ).astype(jnp.bfloat16)
        patched = stale_block.at[redo_index].set(redone)
        image_rows = lax.all_gather(patched, "patch", axis=0, tiled=True)
        normed = modulate(layer_input, mod_rows[0], mod_rows[1])
        projected = jnp.dot(normed, full_qkv, preferred_element_type=jnp.float32).astype(
            jnp.bfloat16
        )
        fresh_rows = projected[:, head_width:]
        image_rows = lax.dynamic_update_slice_in_dim(
            image_rows, fresh_rows, patch_index * patch_rows, 0
        )
        context = jnp.concatenate([text_rows, image_rows], axis=0)
        usable = jnp.concatenate(
            [jnp.arange(text_slots) < text_count, jnp.ones((image_rows.shape[0],), jnp.bool_)]
        )
        attended = attend(
            projected[:, :head_width], context[:, :head_width], context[:, head_width:], usable
        )
        update = jnp.dot(attended, full_out, preferred_element_type=jnp.float32)
        layer_out = (layer_input.astype(jnp.float32) + mod_rows[2] * update).astype(jnp.bfloat16)
        return (layer_out, fresh_rows)

    first_pass = [process(hidden[slot_number], slot_number) for slot_number in range(request_count)]
    first_out = jnp.stack([entry[0] for entry in first_pass])
    first_fresh = jnp.stack([entry[1] for entry in first_pass])
    received = shifted(first_out, "section", 1)
    second_pass = [
        process(received[slot_number], slot_number) for slot_number in range(request_count)
    ]
    second_out = jnp.stack([entry[0] for entry in second_pass])
    second_fresh = jnp.stack([entry[1] for entry in second_pass])
    fresh_all = jnp.where(section_index == 0, first_fresh, second_fresh)
    half_width = model_width // 2
    returned = shifted(second_out[:, :, :half_width], "section", -1)
    own_half = jnp.where(section_index == 0, returned, second_out[:, :, half_width:])
    source_half = lax.dynamic_slice_in_dim(hidden, section_index * half_width, half_width, 2)
    latents = coefficients[:, 0][:, None, None] * source_half.astype(jnp.float32) + coefficients[
        :, 1
    ][:, None, None] * own_half.astype(jnp.float32)
    return (latents, fresh_all[None])


def solution(mesh):
    return jax.shard_map(
        body,
        mesh=mesh,
        in_specs=(
            P("req", "patch", None),
            P("section", ("patch", "req"), None),
            P("section", ("patch", "req"), None),
            P("section", "req", None, None),
            P("section", "req", None, None),
            P("req"),
            P("section", "req", "patch", None),
            P("section", "req", "patch", None),
            P("section", "req", "patch"),
            P("req", None),
        ),
        out_specs=(P("req", "patch", "section"), P("section", "req", "patch", None)),
        check_vma=False,
    )
```

profile of v0, /device:TPU:1, one launch (start us, length us, event | category | flops | bytes accessed | tf_op | source)
XLA Modules:
  0.0 496.8 jit_solution(3415797970322674418)
XLA Ops:
  7.2 1.6 copy.50
  8.9 1.4 copy.54
  10.4 0.9 slice_reduce_fusion.3
  11.3 1.1 convert_reduce_fusion.4
  12.3 1.1 fusion.130
  14.2 1.5 slice_bitcast_fusion
  15.7 140.7 %all-gather.11.cloned.1.call-done = bf16[1,1536,2304]{2,0,1:T(2,128)(2,1)} async-done(((bf16[1,12,2304]{2,0,1:T(2,128)(2,1)}), bf16[1,1536,2304]{2,0,1:T(2,128)(2,1)}) %all-gather.11.cloned.1.call-update) | async-done | bytes 7077904 | tf_op jit(solution)/shard_map/all_gather | solution.py:59
  156.4 9.0 %copy.67 = bf16[1,1536,2304]{2,1,0:T(8,128)(2,1)} copy(bf16[1,1536,2304]{2,0,1:T(2,128)(2,1)} %all-gather.11.cloned.1.call-done) | data formatting | bytes 14155776
  165.4 3.1 fusion.52
  168.5 1.2 scatter_fusion
  169.8 0.9 copy-done.13
  170.7 3.2 fusion.55
  173.9 1.7 scatter_fusion.1
  175.6 0.9 copy-done.12
  179.3 1.2 slice_bitcast_fusion.7
  180.5 91.4 %all-gather.13.cloned.1.call-done = bf16[1,768,1536]{2,0,1:T(2,128)(2,1)} async-done(((bf16[1,6,1536]{2,0,1:T(2,128)(2,1)}), bf16[1,768,1536]{2,0,1:T(2,128)(2,1)}) %all-gather.13.cloned.1.call-update) | async-done | bytes 2359312 | tf_op jit(solution)/shard_map/all_gather | solution.py:60
  271.9 3.0 copy.65
  275.0 5.2 %convolution_convert_fusion.3 = bf16[256,2304]{1,0:T(8,128)(2,1)S(1)} fusion(bf16[1536,2304]{1,0:T(8,128)(2,1)} %bitcast.210, f32[1536]{0:T(1024)S(1)} %get-tuple-element.16, f32[1536]{0:T(1024)S(1)} %get-tuple-element.17, f32[256]{0:T(256)S(1)} %add_rsqrt_fusion.3, f32[256]{0:T(256)S(1)} %broadcast_multiply_fusion.3, bf16[2,256,1536]{2,1,0:T(8,128)(2,1)S(1)} %copy-done.1), kind=kOutput, calls=%fused_computation.46 | convolution fusion | flops 1814888448 | bytes 9062400 | tf_op jit(solution)/shard_map/dot_general | solution.py:84
  280.2 1.0 copy-done.21
  281.2 0.8 slice.169
  282.0 1.9 copy.52
  283.9 5.7 %convolution_convert_fusion.2 = bf16[256,2304]{1,0:T(8,128)(2,1)S(1)} fusion(bf16[1536,2304]{1,0:T(8,128)(2,1)} %bitcast.211, f32[1536]{0:T(1024)S(1)} %get-tuple-element.18, f32[1536]{0:T(1024)S(1)} %get-tuple-element.19, f32[256]{0:T(256)S(1)} %add_rsqrt_fusion.2, f32[256]{0:T(256)S(1)} %broadcast_multiply_fusion.2, bf16[2,256,1536]{2,1,0:T(8,128)(2,1)} %param.10), kind=kOutput, calls=%fused_computation.45 | convolution fusion | flops 1814888448 | bytes 9058304 | tf_op jit(solution)/shard_map/dot_general | solution.py:84
  289.7 1.0 copy-done.19
  291.4 1.9 copy.56
  293.3 23.1 %all-gather.7.cloned.1.call-done = bf16[1024,1536]{1,0:T(8,128)(2,1)} async-done(((bf16[256,1536]{1,0:T(8,128)(2,1)}), bf16[1024,1536]{1,0:T(8,128)(2,1)}) %all-gather.7.cloned.1.call-update) | async-done | bytes 3145744 | tf_op jit(solution)/shard_map/all_gather | solution.py:82
  316.4 3.9 copy.73
  320.3 1.0 slice_bitcast_fusion.5
  321.3 2.1 pad_maximum_fusion.3
  323.4 3.9 copy.53
  327.3 4.0 copy.51
  331.3 29.1 %all-gather.9.cloned.1.call-done = bf16[1024,1536]{1,0:T(8,128)(2,1)} async-done(((bf16[256,1536]{1,0:T(8,128)(2,1)}), bf16[1024,1536]{1,0:T(8,128)(2,1)}) %all-gather.9.cloned.1.call-update) | async-done | bytes 3145744 | tf_op jit(solution)/shard_map/all_gather | solution.py:82
  360.4 3.9 copy.72
  364.3 1.1 slice_bitcast_fusion.4
  365.4 2.0 pad_maximum_fusion.1
  367.4 3.9 copy.57
  371.4 4.1 copy.55
  375.4 6.9 %fusion.178 = f32[12,256]{1,0:T(8,128)S(1)} fusion(pred[1184]{0:T(1024)(128)(4,1)S(1)} %concatenate.35, bf16[256,12,64]{0,2,1:T(8,128)(2,1)} %bitcast.232, bf16[1184,12,64]{0,2,1:T(8,128)(2,1)} %bitcast.216), kind=kOutput, calls=%fused_computation.243 | convolution fusion | flops 480117920 | bytes 2225312 | tf_op jit(solution)/shard_map/sub | solution.py:38
  382.3 9.5 %fusion.93 = bf16[12,64,256]{2,1,0:T(8,128)(2,1)} fusion(bf16[1184,12,64]{0,2,1:T(8,128)(2,1)} %bitcast.218, f32[12,256]{1,0:T(8,128)S(1)} %fusion.178, pred[1184]{0:T(1024)(128)(4,1)S(1)} %concatenate.35, bf16[256,12,64]{0,2,1:T(8,128)(2,1)} %bitcast.233, bf16[1184,12,64]{0,2,1:T(8,128)(2,1)} %bitcast.217), kind=kOutput, calls=%fused_computation.131 | convolution fusion | flops 949522560 | bytes 4437152 | tf_op jit(solution)/shard_map/hqk,khd->qhd/dot_general | solution.py:40
  391.8 7.1 %fusion.177 = f32[12,256]{1,0:T(8,128)S(1)} fusion(pred[1184]{0:T(1024)(128)(4,1)S(1)} %concatenate.37, bf16[256,12,64]{0,2,1:T(8,128)(2,1)} %bitcast.234, bf16[1184,12,64]{0,2,1:T(8,128)(2,1)} %bitcast.223), kind=kOutput, calls=%fused_computation.242 | convolution fusion | flops 480117920 | bytes 2225312 | tf_op jit(solution)/shard_map/sub | solution.py:38
  398.9 9.4 %fusion.92 = bf16[12,64,256]{2,1,0:T(8,128)(2,1)} fusion(bf16[1184,12,64]{0,2,1:T(8,128)(2,1)} %bitcast.227, f32[12,256]{1,0:T(8,128)S(1)} %fusion.177, pred[1184]{0:T(1024)(128)(4,1)S(1)} %concatenate.37, bf16[256,12,64]{0,2,1:T(8,128)(2,1)} %bitcast.235, bf16[1184,12,64]{0,2,1:T(8,128)(2,1)} %bitcast.224), kind=kOutput, calls=%fused_computation.130 | convolution fusion | flops 949522560 | bytes 4437152 | tf_op jit(solution)/shard_map/hqk,khd->qhd/dot_general | solution.py:40
  408.3 2.2 fusion.39
  410.5 2.3 fusion.38
  413.0 1.3 collective-permute-start
  414.3 4.0 collective-permute-done
  419.2 2.2 convolution_convert_fusion
  421.4 1.1 slice_bitcast_fusion.2
  422.7 2.2 convolution_convert_fusion.1
  424.9 1.1 slice_bitcast_fusion.3
  426.0 3.5 pad_maximum_fusion
  429.5 4.0 copy.63
  433.7 4.1 copy.61
  437.7 4.0 copy.60
  441.9 4.1 copy.58
  446.0 6.7 %fusion.180 = f32[12,256]{1,0:T(8,128)S(1)} fusion(pred[1184]{0:T(1024)(128)(4,1)S(1)} %copy-done.30, bf16[256,12,64]{0,2,1:T(8,128)(2,1)S(1)} %bitcast.238, bf16[1184,12,64]{0,2,1:T(8,128)(2,1)} %bitcast.221), kind=kOutput, calls=%fused_computation.245 | convolution fusion | flops 480117920 | bytes 2225312 | tf_op jit(solution)/shard_map/sub | solution.py:38
  452.7 8.7 %fusion.90 = bf16[12,64,256]{2,1,0:T(8,128)(2,1)S(1)} fusion(bf16[1184,12,64]{0,2,1:T(8,128)(2,1)} %bitcast.225, f32[12,256]{1,0:T(8,128)S(1)} %fusion.180, pred[1184]{0:T(1024)(128)(4,1)S(1)} %copy-done.30, bf16[256,12,64]{0,2,1:T(8,128)(2,1)} %bitcast.239, bf16[1184,12,64]{0,2,1:T(8,128)(2,1)} %bitcast.222), kind=kOutput, calls=%fused_computation.128 | convolution fusion | flops 949522560 | bytes 4437152 | tf_op jit(solution)/shard_map/hqk,khd->qhd/dot_general | solution.py:40
  461.4 7.0 %fusion.179 = f32[12,256]{1,0:T(8,128)S(1)} fusion(pred[1184]{0:T(1024)(128)(4,1)S(1)} %copy-done.28, bf16[256,12,64]{0,2,1:T(8,128)(2,1)S(1)} %bitcast.236, bf16[1184,12,64]{0,2,1:T(8,128)(2,1)} %bitcast.219), kind=kOutput, calls=%fused_computation.244 | convolution fusion | flops 480117920 | bytes 2225312 | tf_op jit(solution)/shard_map/sub | solution.py:38
  468.4 9.3 %fusion.91 = bf16[12,64,256]{2,1,0:T(8,128)(2,1)} fusion(bf16[1184,12,64]{0,2,1:T(8,128)(2,1)} %bitcast.226, f32[12,256]{1,0:T(8,128)S(1)} %fusion.179, pred[1184]{0:T(1024)(128)(4,1)S(1)} %copy-done.28, bf16[256,12,64]{0,2,1:T(8,128)(2,1)S(1)} %bitcast.237, bf16[1184,12,64]{0,2,1:T(8,128)(2,1)} %bitcast.220), kind=kOutput, calls=%fused_computation.129 | convolution fusion | flops 949522560 | bytes 4437152 | tf_op jit(solution)/shard_map/hqk,khd->qhd/dot_general | solution.py:40
  477.7 2.1 fusion.36
  479.8 0.8 fusion.37
  480.6 0.9 copy-done.10
  481.5 0.9 fusion.94
  482.4 3.1 collective-permute-start.1
  485.8 2.7 maximum_select_fusion
  488.5 1.6 multiply_add_fusion
  (104 shorter events, 6.3 us)
Async XLA Ops:
  7.2 149.3 %all-gather.11.cloned.1.call-start = ((), (), s32[]{:S(2)}) async-start(), calls=%async_computation.2 | async-start | bytes 14266368 | tf_op jit(solution)/shard_map/all_gather | solution.py:59
  8.8 263.1 %all-gather.13.cloned.1.call-start = ((), (), s32[]{:S(2)}) async-start(), calls=%async_computation.3 | async-start | bytes 4755456 | tf_op jit(solution)/shard_map/all_gather | solution.py:60
  10.3 306.1 %all-gather.7.cloned.1.call-start = ((), (), s32[]{:S(2)}) async-start(), calls=%async_computation | async-start | bytes 3932160 | tf_op jit(solution)/shard_map/all_gather | solution.py:82
  15.7 149.7 %copy-start.23 = (bf16[1,2,24,1536]{3,2,1,0:T(8,128)(2,1)S(1)}, bf16[1,2,24,1536]{3,2,1,0:T(8,128)(2,1)}, u32[]{:S(2)}) copy-start(bf16[1,2,24,1536]{3,2,1,0:T(8,128)(2,1)} %param.17) | copy-start | bytes 442372
  169.7 0.9 copy-start.13
  170.6 189.7 %all-gather.9.cloned.1.call-start = ((), (), s32[]{:S(2)}) async-start(), calls=%async_computation.1 | async-start | bytes 3932160 | tf_op jit(solution)/shard_map/all_gather | solution.py:82
  173.9 2.6 copy-start.31
  173.9 4.5 copy-start
  175.6 0.9 copy-start.12
  177.8 204.5 %copy-start.27 = (pred[1184]{0:T(1024)(128)(4,1)}, pred[1184]{0:T(1024)(128)(4,1)S(1)}, u32[]{:S(2)}) copy-start(pred[1184]{0:T(1024)(128)(4,1)S(1)} %concatenate.35) | copy-start | bytes 3556
  178.4 220.5 %copy-start.29 = (pred[1184]{0:T(1024)(128)(4,1)}, pred[1184]{0:T(1024)(128)(4,1)S(1)}, u32[]{:S(2)}) copy-start(pred[1184]{0:T(1024)(128)(4,1)S(1)} %concatenate.37) | copy-start | bytes 3556
  271.9 3.0 copy-start.1
  280.2 1.0 copy-start.21
  289.6 1.0 copy-start.19
  316.4 3.9 copy-start.6
  316.4 3.9 copy-start.22
  360.4 3.9 copy-start.7
  360.4 3.9 copy-start.20
  408.3 2.2 copy-start.2
  408.3 10.9 %slice-start = ((s8[7077888]{0:T(1024)(128)(4,1)}), s8[4194304]{0:T(1024)(128)(4,1)S(1)}, s32[]{:S(2)}) async-start(s8[7077888]{0:T(1024)(128)(4,1)} %bitcast.212), calls=%async_computation.4 | async-start | bytes 8388608
  410.5 8.7 %slice-start.1 = ((s8[7077888]{0:T(1024)(128)(4,1)}), s8[2883584]{0:T(1024)(128)(4,1)S(1)}, s32[]{:S(2)}) async-start(s8[7077888]{0:T(1024)(128)(4,1)} %bitcast.212), calls=%async_computation.5 | async-start | bytes 5767168
  413.0 5.3 %collective-permute-start = (bf16[2,256,1536]{2,1,0:T(8,128)(2,1)S(1)}, bf16[2,256,1536]{2,1,0:T(8,128)(2,1)S(1)}, u32[]{:S(2)}, u32[]{:S(2)}) collective-permute-start(bf16[2,256,1536]{2,1,0:T(8,128)(2,1)S(1)} %pad_maximum_fusion.4), channel_id=1, source_target_pairs={{0,128},{1,129},{2,130},{3,131},{4,132},{5,133},{6,134},{7,135},{8... | collective-permute-start | bytes 4718600 | tf_op jit(solution)/shard_map/ppermute | solution.py:14
  418.3 4.4 copy-start.4
  419.2 2.2 copy-start.9
  421.4 1.3 copy-start.17
  422.7 2.2 copy-start.8
  424.9 4.6 copy-start.18
  429.5 4.0 slice-start.2
  433.7 12.3 %copy-start.25 = (bf16[256,768]{0,1:T(8,128)(2,1)}, bf16[256,768]{0,1:T(8,128)(2,1)S(1)}, u32[]{:S(2)}) copy-start(bf16[256,768]{0,1:T(8,128)(2,1)S(1)} %copy.62) | copy-start | bytes 1179652
  437.7 4.0 slice-start.3
  441.9 4.1 copy-start.30
  452.7 8.7 %copy-start.28 = (pred[1184]{0:T(1024)(128)(4,1)S(1)}, pred[1184]{0:T(1024)(128)(4,1)}, u32[]{:S(2)}) copy-start(pred[1184]{0:T(1024)(128)(4,1)} %copy-done.27) | copy-start | bytes 3556
  477.7 2.1 copy-start.5
  477.7 2.1 copy-start.24
  480.6 0.9 copy-start.10
  481.5 4.1 copy-start.26
  481.5 4.2 copy-start.14
  481.5 4.2 copy-start.15
  481.5 4.3 copy-start.16
  482.4 6.0 %collective-permute-start.1 = (bf16[2,256,768]{2,1,0:T(8,128)(2,1)}, bf16[2,256,768]{2,1,0:T(8,128)(2,1)}, u32[]{:S(2)}, u32[]{:S(2)}) collective-permute-start(bf16[2,256,768]{2,1,0:T(8,128)(2,1)} %fusion.94), channel_id=1, source_target_pairs={{128,0},{129,1},{130,2},{131,3},{132,4},{133,5},{134,6},{135,7},{1... | collective-permute-start | bytes 2359304 | tf_op jit(solution)/shard_map/ppermute | solution.py:14
  485.7 2.7 copy-start.3
  485.7 2.7 copy-start.11
Sparse Core Ops, SparseCore 0:
  12.3 144.0 all-gather.10
  160.8 111.1 all-gather.12
  273.7 42.6 all-gather.6
  318.1 42.2 all-gather.8
where the time goes:
time: 502 us; the launch traced here: 497 us
  waiting for transfers between devices  288 us (57%)
  matrix products  93.5 us (19%)
  local copies, waits for them, and re-layouts  76.1 us (15%)
  other arithmetic  19.8 us (4%)
  between operations  14.6 us (3%)
    all_gather x1, waiting for transfers between devices, body(): lax.all_gather(w_qkv[0], ('patch', 'req'), axis=0, tiled=True)  141 us
    all_gather x1, waiting for transfers between devices, body(): lax.all_gather(w_out[0], ('patch', 'req'), axis=0, tiled=True)  91.4 us
    all_gather x2, waiting for transfers between devices, process(): image_rows = lax.all_gather(patched, 'patch', axis=0, tiled=True)  52.2 us
    dot_general x4, matrix products, attend(): jnp.einsum('hqk,khd->qhd', soft_weights, value_heads, preferred_element_t...  36.9 us
    unnamed x74, local copies, waits for them, and re-layouts  27.8 us
    sub x4, matrix products, attend(): exp_scores = jnp.exp(scores - row_max)  27.6 us
    slice x4, local copies, waits for them, and re-layouts, process(): context[:, head_width:]  16.2 us
    slice x4, local copies, waits for them, and re-layouts, process(): context[:, :head_width]  15.8 us
  transfers between devices with their start and end apart: 6, of which 5 were waited for; matrix products, arithmetic and copies ran while one was open for 13% of the time, Pallas kernels for 0%

commit v1 on v0

--- a/solution.py
+++ b/solution.py
@@ -6,6 +6,11 @@
 HEADS = 12
 norm_eps = 1e-06
 score_scale = 0.125
+
+
+def gather_from_all(x, axis, dim):
+    copies = jnp.concatenate([x] * lax.axis_size(axis), axis=dim)
+    return lax.all_to_all(copies, axis, dim, dim, tiled=True)
 
 
 def shifted(block, axis, distance):
@@ -79,7 +84,7 @@
             held_norm, full_qkv[:, head_width:], preferred_element_type=jnp.float32
         ).astype(jnp.bfloat16)
         patched = stale_block.at[redo_index].set(redone)
-        image_rows = lax.all_gather(patched, "patch", axis=0, tiled=True)
+        image_rows = gather_from_all(patched, "patch", 0)
         normed = modulate(layer_input, mod_rows[0], mod_rows[1])
         projected = jnp.dot(normed, full_qkv, preferred_element_type=jnp.float32).astype(
             jnp.bfloat16

time: 502 us -> 456 us (0.908)
  waiting for transfers between devices: 288 us -> 225 us
  other arithmetic: 19.8 us -> 29.1 us
  starting transfers between devices: 4.55 us -> 13.5 us
    all_gather x2 -> x0, waiting for transfers between devices: 52.2 us -> none  [process(): image_rows = lax.all_gather(patched, 'patch', axis=0, tiled=True)]
    all_gather x1, waiting for transfers between devices: 91.4 us -> 57.5 us  [body(): lax.all_gather(w_out[0], ('patch', 'req'), axis=0, tiled=True)]
    all_to_all x0 -> x2, waiting for transfers between devices: none -> 23.1 us  [gather_from_all(): return lax.all_to_all(copies, axis, dim, dim, tiled=True)]
    all_to_all x0 -> x2, starting transfers between devices: none -> 9.07 us  [gather_from_all(): return lax.all_to_all(copies, axis, dim, dim, tiled=True)]
    concatenate x0 -> x2, other arithmetic: none -> 5.34 us  [gather_from_all(): copies = jnp.concatenate([x] * lax.axis_size(axis), axis=dim)]
    unnamed x74 -> x76, local copies, waits for them, and re-layouts: 27.8 us -> 27.8 us
  transfers between devices with their start and end apart: 6 -> 6, of which waited for: 5 -> 4; matrix products, arithmetic and copies ran while one was open for 13% -> 16% of each run, Pallas kernels for 0% -> 0%
where the time goes in v1:
time: 456 us; the launch traced here: 450 us
  waiting for transfers between devices  225 us (49%)
  matrix products  93.1 us (20%)
  local copies, waits for them, and re-layouts  74.1 us (16%)
  other arithmetic  29.1 us (6%)
  between operations  14.9 us (3%)
  starting transfers between devices  13.5 us (3%)
    all_gather x1, waiting for transfers between devices, body(): lax.all_gather(w_qkv[0], ('patch', 'req'), axis=0, tiled=True)  138 us
    all_gather x1, waiting for transfers between devices, body(): lax.all_gather(w_out[0], ('patch', 'req'), axis=0, tiled=True)  57.5 us
    dot_general x4, matrix products, attend(): jnp.einsum('hqk,khd->qhd', soft_weights, value_heads, preferred_element_t...  36.9 us
    unnamed x76, local copies, waits for them, and re-layouts  27.8 us
    sub x4, matrix products, attend(): exp_scores = jnp.exp(scores - row_max)  27.6 us
    all_to_all x2, waiting for transfers between devices, gather_from_all(): return lax.all_to_all(copies, axis, dim, dim, tiled=True)  23.1 us
    slice x4, local copies, waits for them, and re-layouts, process(): context[:, head_width:]  16.2 us
    slice x4, local copies, waits for them, and re-layouts, process(): context[:, :head_width]  15.8 us
  transfers between devices with their start and end apart: 6, of which 4 were waited for; matrix products, arithmetic and copies ran while one was open for 16% of the time, Pallas kernels for 0%

profile of v1, /device:TPU:1, one launch (start us, length us, event | category | flops | bytes accessed | tf_op | source)
XLA Modules:
  0.0 449.9 jit_solution(6251086296014955691)
XLA Ops:
  7.2 1.7 copy.50
  9.0 1.4 copy.54
  11.3 1.1 convert_reduce_fusion.4
  12.4 1.3 fusion.176
  13.7 1.1 fusion.130
  15.5 1.7 convert_reduce_fusion.3
  17.2 1.0 slice_bitcast_fusion
  18.2 138.2 %all-gather.5.cloned.1.call-done = bf16[1,1536,2304]{2,0,1:T(2,128)(2,1)} async-done(((bf16[1,12,2304]{2,0,1:T(2,128)(2,1)}), bf16[1,1536,2304]{2,0,1:T(2,128)(2,1)}) %all-gather.5.cloned.1.call-update) | async-done | bytes 7077904 | tf_op jit(solution)/shard_map/all_gather | solution.py:64
  156.4 9.0 %copy.67 = bf16[1,1536,2304]{2,1,0:T(8,128)(2,1)} copy(bf16[1,1536,2304]{2,0,1:T(2,128)(2,1)} %all-gather.5.cloned.1.call-done) | data formatting | bytes 14155776
  165.4 3.1 fusion.52
  168.6 1.2 scatter_fusion
  169.8 1.8 pad_maximum_fusion
  171.6 4.0 all-to-all-start
  176.3 2.0 fusion.86
  178.3 1.1 slice_bitcast_fusion.7
  179.4 3.1 fusion.55
  182.5 2.9 scatter_fusion.1
  185.4 3.5 pad_maximum_fusion.1
  188.9 23.1 %all-to-all-done = bf16[4,256,1536]{2,1,0:T(8,128)(2,1)S(1)} async-done(((bf16[4,256,1536]{2,1,0:T(8,128)(2,1)}), bf16[4,256,1536]{2,1,0:T(8,128)(2,1)S(1)}, u32[]{:S(2)}, u32[]{:S(2)}) %all-to-all-start) | async-done | bytes 3145760 | tf_op jit(solution)/shard_map/all_to_all | solution.py:13
  212.0 1.6 copy-done
  213.6 5.1 %all-to-all-start.1 = ((bf16[4,256,1536]{2,1,0:T(8,128)(2,1)}), bf16[4,256,1536]{2,1,0:T(8,128)(2,1)}, u32[]{:S(2)}, u32[]{:S(2)}) async-start(bf16[4,256,1536]{2,1,0:T(8,128)(2,1)} %bitcast.215), calls=%async_computation.1 | async-start | bytes 6291456 | tf_op jit(solution)/shard_map/all_to_all | solution.py:13
  218.7 57.5 %all-gather.7.cloned.1.call-done = bf16[1,768,1536]{2,0,1:T(2,128)(2,1)} async-done(((bf16[1,6,1536]{2,0,1:T(2,128)(2,1)}), bf16[1,768,1536]{2,0,1:T(2,128)(2,1)}) %all-gather.7.cloned.1.call-update) | async-done | bytes 2359312 | tf_op jit(solution)/shard_map/all_gather | solution.py:65
  276.2 3.0 copy.65
  279.2 5.2 %convolution_convert_fusion.3 = bf16[256,2304]{1,0:T(8,128)(2,1)S(1)} fusion(bf16[1536,2304]{1,0:T(8,128)(2,1)} %bitcast.218, f32[1536]{0:T(1024)S(1)} %get-tuple-element.16, f32[1536]{0:T(1024)S(1)} %get-tuple-element.17, f32[256]{0:T(256)S(1)} %add_rsqrt_fusion.3, f32[256]{0:T(256)S(1)} %broadcast_multiply_fusion.3, bf16[2,256,1536]{2,1,0:T(8,128)(2,1)S(1)} %copy-done.2), kind=kOutput, calls=%fused_computation.46 | convolution fusion | flops 1814888448 | bytes 9062400 | tf_op jit(solution)/shard_map/dot_general | solution.py:89
  284.4 1.0 copy-done.21
  286.4 5.4 %convolution_convert_fusion.2 = bf16[256,2304]{1,0:T(8,128)(2,1)S(1)} fusion(bf16[1536,2304]{1,0:T(8,128)(2,1)} %bitcast.219, f32[1536]{0:T(1024)S(1)} %get-tuple-element.18, f32[1536]{0:T(1024)S(1)} %get-tuple-element.19, f32[256]{0:T(256)S(1)} %add_rsqrt_fusion.2, f32[256]{0:T(256)S(1)} %broadcast_multiply_fusion.2, bf16[2,256,1536]{2,1,0:T(8,128)(2,1)} %param.10), kind=kOutput, calls=%fused_computation.45 | convolution fusion | flops 1814888448 | bytes 9058304 | tf_op jit(solution)/shard_map/dot_general | solution.py:89
  291.8 1.0 copy-done.19
  292.8 0.9 copy.56
  293.7 3.9 copy.73
  297.7 1.0 slice_bitcast_fusion.5
  298.7 2.1 pad_maximum_fusion.5
  300.8 3.9 copy.53
  304.7 3.9 copy.51
  308.7 3.9 copy.72
  312.6 1.3 slice_bitcast_fusion.4
  313.8 3.9 pad_maximum_fusion.3
  317.8 3.9 copy.57
  321.7 4.1 copy.55
  325.8 6.9 %fusion.178 = f32[12,256]{1,0:T(8,128)S(1)} fusion(pred[1184]{0:T(1024)(128)(4,1)S(1)} %concatenate.44, bf16[256,12,64]{0,2,1:T(8,128)(2,1)} %bitcast.240, bf16[1184,12,64]{0,2,1:T(8,128)(2,1)} %bitcast.224), kind=kOutput, calls=%fused_computation.245 | convolution fusion | flops 480117920 | bytes 2225312 | tf_op jit(solution)/shard_map/sub | solution.py:43
  332.6 9.4 %fusion.93 = bf16[12,64,256]{2,1,0:T(8,128)(2,1)} fusion(bf16[1184,12,64]{0,2,1:T(8,128)(2,1)} %bitcast.226, f32[12,256]{1,0:T(8,128)S(1)} %fusion.178, pred[1184]{0:T(1024)(128)(4,1)S(1)} %concatenate.44, bf16[256,12,64]{0,2,1:T(8,128)(2,1)} %bitcast.241, bf16[1184,12,64]{0,2,1:T(8,128)(2,1)} %bitcast.225), kind=kOutput, calls=%fused_computation.133 | convolution fusion | flops 949522560 | bytes 4437152 | tf_op jit(solution)/shard_map/hqk,khd->qhd/dot_general | solution.py:45
  342.1 7.1 %fusion.177 = f32[12,256]{1,0:T(8,128)S(1)} fusion(pred[1184]{0:T(1024)(128)(4,1)S(1)} %concatenate.47, bf16[256,12,64]{0,2,1:T(8,128)(2,1)} %bitcast.242, bf16[1184,12,64]{0,2,1:T(8,128)(2,1)} %bitcast.231), kind=kOutput, calls=%fused_computation.244 | convolution fusion | flops 480117920 | bytes 2225312 | tf_op jit(solution)/shard_map/sub | solution.py:43
  349.2 9.5 %fusion.92 = bf16[12,64,256]{2,1,0:T(8,128)(2,1)} fusion(bf16[1184,12,64]{0,2,1:T(8,128)(2,1)} %bitcast.235, f32[12,256]{1,0:T(8,128)S(1)} %fusion.177, pred[1184]{0:T(1024)(128)(4,1)S(1)} %concatenate.47, bf16[256,12,64]{0,2,1:T(8,128)(2,1)} %bitcast.243, bf16[1184,12,64]{0,2,1:T(8,128)(2,1)} %bitcast.232), kind=kOutput, calls=%fused_computation.132 | convolution fusion | flops 949522560 | bytes 4437152 | tf_op jit(solution)/shard_map/hqk,khd->qhd/dot_general | solution.py:45
  358.6 2.2 fusion.39
  360.9 2.3 fusion.38
  363.4 1.3 collective-permute-start
  364.7 6.5 %collective-permute-done = bf16[2,256,1536]{2,1,0:T(8,128)(2,1)S(1)} collective-permute-done((bf16[2,256,1536]{2,1,0:T(8,128)(2,1)S(1)}, bf16[2,256,1536]{2,1,0:T(8,128)(2,1)S(1)}, u32[]{:S(2)}, u32[]{:S(2)}) %collective-permute-start) | collective-permute-done | bytes 1572896 | tf_op jit(solution)/shard_map/ppermute | solution.py:19
  372.1 2.2 convolution_convert_fusion
  374.3 1.1 slice_bitcast_fusion.2
  375.5 2.2 convolution_convert_fusion.1
  377.7 1.1 slice_bitcast_fusion.3
  378.8 3.5 pad_maximum_fusion.2
  382.3 4.0 copy.63
  386.5 4.1 copy.61
  390.6 4.0 copy.60
  394.7 4.1 copy.58
  398.8 6.7 %fusion.180 = f32[12,256]{1,0:T(8,128)S(1)} fusion(pred[1184]{0:T(1024)(128)(4,1)S(1)} %copy-done.31, bf16[256,12,64]{0,2,1:T(8,128)(2,1)S(1)} %bitcast.246, bf16[1184,12,64]{0,2,1:T(8,128)(2,1)} %bitcast.229), kind=kOutput, calls=%fused_computation.247 | convolution fusion | flops 480117920 | bytes 2225312 | tf_op jit(solution)/shard_map/sub | solution.py:43
  405.5 8.7 %fusion.90 = bf16[12,64,256]{2,1,0:T(8,128)(2,1)S(1)} fusion(bf16[1184,12,64]{0,2,1:T(8,128)(2,1)} %bitcast.233, f32[12,256]{1,0:T(8,128)S(1)} %fusion.180, pred[1184]{0:T(1024)(128)(4,1)S(1)} %copy-done.31, bf16[256,12,64]{0,2,1:T(8,128)(2,1)} %bitcast.247, bf16[1184,12,64]{0,2,1:T(8,128)(2,1)} %bitcast.230), kind=kOutput, calls=%fused_computation.130 | convolution fusion | flops 949522560 | bytes 4437152 | tf_op jit(solution)/shard_map/hqk,khd->qhd/dot_general | solution.py:45
  414.3 7.0 %fusion.179 = f32[12,256]{1,0:T(8,128)S(1)} fusion(pred[1184]{0:T(1024)(128)(4,1)S(1)} %copy-done.29, bf16[256,12,64]{0,2,1:T(8,128)(2,1)S(1)} %bitcast.244, bf16[1184,12,64]{0,2,1:T(8,128)(2,1)} %bitcast.227), kind=kOutput, calls=%fused_computation.246 | convolution fusion | flops 480117920 | bytes 2225312 | tf_op jit(solution)/shard_map/sub | solution.py:43
  421.2 9.3 %fusion.91 = bf16[12,64,256]{2,1,0:T(8,128)(2,1)} fusion(bf16[1184,12,64]{0,2,1:T(8,128)(2,1)} %bitcast.234, f32[12,256]{1,0:T(8,128)S(1)} %fusion.179, pred[1184]{0:T(1024)(128)(4,1)S(1)} %copy-done.29, bf16[256,12,64]{0,2,1:T(8,128)(2,1)S(1)} %bitcast.245, bf16[1184,12,64]{0,2,1:T(8,128)(2,1)} %bitcast.228), kind=kOutput, calls=%fused_computation.131 | convolution fusion | flops 949522560 | bytes 4437152 | tf_op jit(solution)/shard_map/hqk,khd->qhd/dot_general | solution.py:45
  430.5 2.1 fusion.36
  434.3 0.9 fusion.94
  435.3 3.1 collective-permute-start.1
  438.6 2.7 maximum_select_fusion
  441.3 1.6 multiply_add_fusion
  (106 shorter events, 6.8 us)
Async XLA Ops:
  7.2 10.0 %copy-start.32 = (s32[1,2,24]{2,1,0:T(2,128)S(1)}, s32[1,2,24]{2,1,0:T(2,128)}, u32[]{:S(2)}) copy-start(s32[1,2,24]{2,1,0:T(2,128)} %param.18) | copy-start | bytes 580
  7.2 10.1 %copy-start.16 = (bf16[1,2,256,1536]{3,2,1,0:T(8,128)(2,1)S(1)}, bf16[1,2,256,1536]{3,2,1,0:T(8,128)(2,1)}, u32[]{:S(2)}) copy-start(bf16[1,2,256,1536]{3,2,1,0:T(8,128)(2,1)} %param.16) | copy-start | bytes 4718596
  7.2 149.3 %all-gather.5.cloned.1.call-start = ((), (), s32[]{:S(2)}) async-start(), calls=%async_computation.2 | async-start | bytes 14266368 | tf_op jit(solution)/shard_map/all_gather | solution.py:64
  9.0 267.2 %all-gather.7.cloned.1.call-start = ((), (), s32[]{:S(2)}) async-start(), calls=%async_computation.3 | async-start | bytes 4755456 | tf_op jit(solution)/shard_map/all_gather | solution.py:65
  18.2 147.2 %copy-start.24 = (bf16[1,2,24,1536]{3,2,1,0:T(8,128)(2,1)S(1)}, bf16[1,2,24,1536]{3,2,1,0:T(8,128)(2,1)}, u32[]{:S(2)}) copy-start(bf16[1,2,24,1536]{3,2,1,0:T(8,128)(2,1)} %param.17) | copy-start | bytes 442372
  171.6 40.4 %all-to-all-start = ((bf16[4,256,1536]{2,1,0:T(8,128)(2,1)}), bf16[4,256,1536]{2,1,0:T(8,128)(2,1)S(1)}, u32[]{:S(2)}, u32[]{:S(2)}) async-start(bf16[4,256,1536]{2,1,0:T(8,128)(2,1)} %bitcast.214), calls=%async_computation | async-start | bytes 6291456 | tf_op jit(solution)/shard_map/all_to_all | solution.py:13
  176.2 156.4 %copy-start.28 = (pred[1184]{0:T(1024)(128)(4,1)}, pred[1184]{0:T(1024)(128)(4,1)S(1)}, u32[]{:S(2)}) copy-start(pred[1184]{0:T(1024)(128)(4,1)S(1)} %concatenate.44) | copy-start | bytes 3556
  176.2 173.0 %copy-start.30 = (pred[1184]{0:T(1024)(128)(4,1)}, pred[1184]{0:T(1024)(128)(4,1)S(1)}, u32[]{:S(2)}) copy-start(pred[1184]{0:T(1024)(128)(4,1)S(1)} %concatenate.47) | copy-start | bytes 3556
  176.2 2.1 copy-start.23
  212.0 1.6 copy-start
  213.6 95.1 %all-to-all-start.1 = ((bf16[4,256,1536]{2,1,0:T(8,128)(2,1)}), bf16[4,256,1536]{2,1,0:T(8,128)(2,1)}, u32[]{:S(2)}, u32[]{:S(2)}) async-start(bf16[4,256,1536]{2,1,0:T(8,128)(2,1)} %bitcast.215), calls=%async_computation.1 | async-start | bytes 6291456 | tf_op jit(solution)/shard_map/all_to_all | solution.py:13
  276.2 3.0 copy-start.2
  284.4 1.0 copy-start.21
  291.8 1.0 copy-start.19
  293.7 3.9 copy-start.1
  293.7 3.9 copy-start.22
  297.7 1.1 copy-start.11
  308.7 3.9 copy-start.20
  312.6 1.3 copy-start.12
  358.6 2.2 copy-start.3
  358.6 13.4 %slice-start = ((s8[7077888]{0:T(1024)(128)(4,1)}), s8[4194304]{0:T(1024)(128)(4,1)S(1)}, s32[]{:S(2)}) async-start(s8[7077888]{0:T(1024)(128)(4,1)} %bitcast.220), calls=%async_computation.4 | async-start | bytes 8388608
  360.9 11.2 %slice-start.1 = ((s8[7077888]{0:T(1024)(128)(4,1)}), s8[2883584]{0:T(1024)(128)(4,1)S(1)}, s32[]{:S(2)}) async-start(s8[7077888]{0:T(1024)(128)(4,1)} %bitcast.220), calls=%async_computation.5 | async-start | bytes 5767168
  363.4 7.8 %collective-permute-start = (bf16[2,256,1536]{2,1,0:T(8,128)(2,1)S(1)}, bf16[2,256,1536]{2,1,0:T(8,128)(2,1)S(1)}, u32[]{:S(2)}, u32[]{:S(2)}) collective-permute-start(bf16[2,256,1536]{2,1,0:T(8,128)(2,1)S(1)} %pad_maximum_fusion.6), channel_id=1, source_target_pairs={{0,128},{1,129},{2,130},{3,131},{4,132},{5,133},{6,134},{7,135},{8... | collective-permute-start | bytes 4718600 | tf_op jit(solution)/shard_map/ppermute | solution.py:19
  371.1 4.4 copy-start.5
  372.0 2.2 copy-start.8
  374.2 1.3 copy-start.17
  375.5 2.2 copy-start.7
  377.7 4.6 %copy-start.18 = (bf16[256,2304]{1,0:T(8,128)(2,1)}, bf16[256,2304]{1,0:T(8,128)(2,1)S(1)}, u32[]{:S(2)}) copy-start(bf16[256,2304]{1,0:T(8,128)(2,1)S(1)} %convolution_convert_fusion.1) | copy-start | bytes 3538948
  382.3 4.0 slice-start.2
  386.5 12.3 %copy-start.26 = (bf16[256,768]{0,1:T(8,128)(2,1)}, bf16[256,768]{0,1:T(8,128)(2,1)S(1)}, u32[]{:S(2)}) copy-start(bf16[256,768]{0,1:T(8,128)(2,1)S(1)} %copy.62) | copy-start | bytes 1179652
  390.6 4.0 slice-start.3
  394.7 4.1 copy-start.31
  405.5 8.7 %copy-start.29 = (pred[1184]{0:T(1024)(128)(4,1)S(1)}, pred[1184]{0:T(1024)(128)(4,1)}, u32[]{:S(2)}) copy-start(pred[1184]{0:T(1024)(128)(4,1)} %copy-done.28) | copy-start | bytes 3556
  430.5 2.1 copy-start.6
  430.5 2.1 copy-start.25
  433.4 0.9 copy-start.9
  434.3 4.1 copy-start.27
  434.3 4.2 copy-start.13
  434.3 4.2 copy-start.14
  434.3 4.2 copy-start.15
  435.3 6.0 %collective-permute-start.1 = (bf16[2,256,768]{2,1,0:T(8,128)(2,1)}, bf16[2,256,768]{2,1,0:T(8,128)(2,1)}, u32[]{:S(2)}, u32[]{:S(2)}) collective-permute-start(bf16[2,256,768]{2,1,0:T(8,128)(2,1)} %fusion.94), channel_id=1, source_target_pairs={{128,0},{129,1},{130,2},{131,3},{132,4},{133,5},{134,6},{135,7},{1... | collective-permute-start | bytes 2359304 | tf_op jit(solution)/shard_map/ppermute | solution.py:19
  438.6 2.7 copy-start.4
  438.6 2.7 copy-start.10
Sparse Core Ops, SparseCore 0:
  12.3 144.0 all-gather.4
  160.2 115.9 all-gather.6
